TPU v7x, 32 devices: a whole 2x2x4 slice. The times are simulated.
32 devices in a mesh: dp: 4 (over z), ctx: 8 (over y, x, core).
Axes of the slice: x: 2, y: 2, z: 4, core: 2. Of those that a mesh axis runs over, the one named last changes fastest.
Arguments:
- mixed: bfloat16 [4, 1024, 4096], P('dp', 'ctx'), may hold values from -6 to 6
- conv_weight: float32 [4, 4096], replicated, may hold values from -3 to 3
- log_decay: float32 [4, 1024, 16], P('dp', 'ctx'), may hold values from -1 to 0
- write_rate: float32 [4, 1024, 16], P('dp', 'ctx'), may hold values from 0.1 to 0.95
- segment_ids: int32 [4, 1024], P('dp', 'ctx'), may hold values from 0 to 3, never falling along the last dimension, each value on 1 to 512 neighbouring positions
- cotangent: bfloat16 [4, 1024, 2048], P('dp', 'ctx'), may hold values from -6 to 6
Outputs:
- core_out: bfloat16 [4, 1024, 2048], P('dp', 'ctx')
- grad_mixed: bfloat16 [4, 1024, 4096], P('dp', 'ctx')
- grad_decay: float32 [4, 1024, 16], P('dp', 'ctx')
- grad_rate: float32 [4, 1024, 16], P('dp', 'ctx')
- grad_conv: float32 [4, 4096], replicated
Inputs may be any that keep to these rules, and one draw needn't show every extreme that they name: `segment_ids`: per sequence, segment numbers never fall along the positions; every number of 0 to 3 occurs, each on at most 512 positions.
All inputs are finite; a program needn't handle non-finite values.
Results may differ from a plain program's by a relative error of at most 0.00105.
Values may be sent and summed in bfloat16 or wider, within the bound.
No kernel may reach another device: no remote copies, remote signals or barrier semaphores. Data moves between devices by JAX's collectives and lax.ppermute only.
A program may use at most 320 MiB of HBM per device.

v0:
```python
import math

import jax
import jax.numpy as jnp
from jax import lax
from jax.sharding import PartitionSpec as P

HK = 8
HV = 16
DK = 128
DV = 128
BLOCK = 64


HIGHEST = lax.Precision.HIGHEST


def from_behind(x, axis, by):
    size = lax.axis_size(axis)
    pairs = [(i, i + by) for i in range(size) if 0 <= i + by < size]
    return lax.ppermute(x, axis, pairs)


def prefix(value, axis, join, neutral, backward):
    count, mine = (lax.axis_size(axis), lax.axis_index(axis))
    pieces = jax.tree.map(lambda part: lax.all_gather(part, axis), value)
    if backward:
        pieces = jax.tree.map(lambda part: part[::-1], pieces)
        mine = count - 1 - mine
    total = jax.tree.map(
        lambda part, zero: jnp.full_like(part, 0) + jnp.asarray(zero, part.dtype), value, neutral
    )

    def hop(position, total):
        longer = join(total, jax.tree.map(lambda part: part[position], pieces))
        return jax.tree.map(lambda new, old: jnp.where(position < mine, new, old), longer, total)

    return lax.fori_loop(0, count - 1, hop, total)


def prepare(mix_ext, seg_ext, conv_weight):
    margin = conv_weight.shape[0] - 1
    positions = mix_ext.shape[0] - margin
    current = seg_ext[margin:]
    summed = jnp.zeros((positions, mix_ext.shape[1]), jnp.float32)
    for tap_index in range(margin + 1):
        same_doc = (seg_ext[tap_index : tap_index + positions] == current).astype(jnp.float32)
        summed = (
            summed
            + conv_weight[tap_index][None, :]
            * mix_ext[tap_index : tap_index + positions]
            * same_doc[:, None]
        )
    activated = jax.nn.silu(summed)
    split_at = HK * DK
    queries = activated[:, :split_at].reshape(positions, HK, DK)
    keyset = activated[:, split_at : 2 * split_at].reshape(positions, HK, DK)
    values = activated[:, 2 * split_at :].reshape(positions, HV, DV)
    queries = (
        queries
        / jnp.sqrt(jnp.sum(queries * queries, axis=-1, keepdims=True) + 1e-06)
        / math.sqrt(DK)
    )
    keyset = keyset / jnp.sqrt(jnp.sum(keyset * keyset, axis=-1, keepdims=True) + 1e-06)
    repeats = HV // HK
    return (jnp.repeat(queries, repeats, axis=1), jnp.repeat(keyset, repeats, axis=1), values)


def unit_lower_inverse(strict_part):
    positions = strict_part.shape[-1]
    identity_matrix = jnp.eye(positions, dtype=jnp.float32)[None]
    result = identity_matrix - strict_part
    power = strict_part
    reach = 2
    while reach < positions:
        power = jnp.einsum("hij,hjk->hik", power, power, precision=HIGHEST)
        result = jnp.einsum("hij,hjk->hik", result, identity_matrix + power, precision=HIGHEST)
        reach = reach * 2
    return result


def block_parts(queries, keyset, values, log_decay, write_rate, segments, seg_before):
    positions = queries.shape[0]
    cumulative = jnp.cumsum(log_decay, axis=0)
    keep_state = (segments == seg_before).astype(jnp.float32)
    entering = jnp.exp(cumulative) * keep_state[:, None]
    token_position = lax.iota(jnp.int32, positions)
    same_doc = segments[:, None] == segments[None, :]
    strict = same_doc & (token_position[:, None] > token_position[None, :])
    causal = same_doc & (token_position[:, None] >= token_position[None, :])
    spread = cumulative.T[:, :, None] - cumulative.T[:, None, :]
    strict_decay = jnp.where(strict[None], jnp.exp(jnp.where(strict[None], spread, 0.0)), 0.0)
    causal_decay = jnp.where(causal[None], jnp.exp(jnp.where(causal[None], spread, 0.0)), 0.0)
    key_inner = jnp.einsum("ihd,jhd->hij", keyset, keyset, precision=HIGHEST)
    inverse = unit_lower_inverse(write_rate.T[:, :, None] * key_inner * strict_decay)
    targets = jnp.concatenate(
        [keyset * (write_rate * entering)[:, :, None], values * write_rate[:, :, None]], axis=2
    )
    solved = jnp.einsum("hij,hjd->hid", inverse, targets.transpose(1, 0, 2), precision=HIGHEST)
    write_keys = solved[:, :, :DK]
    write_values = solved[:, :, DK:]
    scores = jnp.einsum("ihd,jhd->hij", queries, keyset, precision=HIGHEST) * causal_decay
    final_sum = cumulative[-1]
    tail_decay = (
        jnp.exp(final_sum[None, :] - cumulative)
        * (segments == segments[-1]).astype(jnp.float32)[:, None]
    )
    carried = jnp.exp(final_sum) * keep_state[-1]
    tail_keys = (keyset * tail_decay[:, :, None]).transpose(1, 0, 2)
    queried = (queries * entering[:, :, None]).transpose(1, 0, 2)
    return (write_keys, write_values, scores, tail_keys, queried, carried)


def block_map(block_data):
    write_keys, write_values, scores, tail_keys, queried, carried = block_data
    identity_matrix = jnp.eye(DK, dtype=jnp.float32)
    transform = carried[:, None, None] * identity_matrix[None] - jnp.einsum(
        "hcd,hce->hde", tail_keys, write_keys, precision=HIGHEST
    )
    shift_term = jnp.einsum("hcd,hce->hde", tail_keys, write_values, precision=HIGHEST)
    return (transform, shift_term)


def block_apply(block_data, state_in):
    write_keys, write_values, scores, tail_keys, queried, carried = block_data
    fresh_values = write_values - jnp.einsum(
        "hcd,hde->hce", write_keys, state_in, precision=HIGHEST
    )
    output = jnp.einsum("hcd,hde->hce", queried, state_in, precision=HIGHEST)
    output = output + jnp.einsum("hij,hje->hie", scores, fresh_values, precision=HIGHEST)
    state_next = carried[:, None, None] * state_in + jnp.einsum(
        "hcd,hce->hde", tail_keys, fresh_values, precision=HIGHEST
    )
    return (output, state_next)


def section_one(mix_ext, conv_weight, log_decay, write_rate, seg_ext):
    queries, keyset, values = prepare(mix_ext, seg_ext, conv_weight)
    margin = conv_weight.shape[0] - 1
    positions = log_decay.shape[0]
    blocks = positions // BLOCK
    segments = seg_ext[margin:]
    before = seg_ext[margin - 1 : margin - 1 + positions : BLOCK]

    def blocked(tensor):
        return tensor.reshape((blocks, BLOCK) + tensor.shape[1:])

    return jax.vmap(block_parts)(
        blocked(queries),
        blocked(keyset),
        blocked(values),
        blocked(log_decay),
        blocked(write_rate),
        blocked(segments),
        before,
    )


def section_two(parts, state_in):

    def step_block(state_now, block_data):
        output, state_next = block_apply(block_data, state_now)
        return (state_next, output)

    state_out, outputs = lax.scan(step_block, state_in, parts)
    blocks = outputs.shape[0]
    return (outputs.transpose(0, 2, 1, 3).reshape(blocks * BLOCK, HV * DV), state_out)


def summarize(parts):
    identity_matrix = jnp.eye(DK, dtype=jnp.float32)
    initial = (
        jnp.broadcast_to(identity_matrix, (HV, DK, DK)),
        jnp.zeros((HV, DK, DV), jnp.float32),
    )

    def fold_block(carried_map, block_data):
        transform, shift_term = block_map(block_data)
        merged = jnp.einsum("hij,hjk->hik", transform, carried_map[0], precision=HIGHEST)
        moved = (
            jnp.einsum("hij,hjk->hik", transform, carried_map[1], precision=HIGHEST) + shift_term
        )
        return ((merged, moved), None)

    result, unused = lax.scan(fold_block, initial, parts)
    return result


def compose(earlier_map, later_map):
    merged = jnp.einsum("shij,shjk->shik", later_map[0], earlier_map[0], precision=HIGHEST)
    moved = (
        jnp.einsum("shij,shjk->shik", later_map[0], earlier_map[1], precision=HIGHEST)
        + later_map[1]
    )
    return (merged, moved)


def local(mixed, conv_weight, log_decay, write_rate, segment_ids, cotangent):
    margin = conv_weight.shape[0] - 1
    shifted_rows, shifted_segs = from_behind(
        (mixed[:, -margin:, :], segment_ids[:, -margin:].astype(jnp.bfloat16)), "ctx", 1
    )
    mix_ext = jnp.concatenate([shifted_rows, mixed], axis=1).astype(jnp.float32)
    seg_ext = jnp.concatenate([shifted_segs.astype(jnp.int32), segment_ids], axis=1)

    def first_section(mix_in, weight_in, decay_in, rate_in):
        return jax.vmap(section_one, in_axes=(0, None, 0, 0, 0))(
            mix_in, weight_in, decay_in, rate_in, seg_ext
        )

    parts, first_pull = jax.vjp(first_section, mix_ext, conv_weight, log_decay, write_rate)
    transform, shift_term = jax.vmap(summarize)(parts)
    identity_pair = (
        jnp.broadcast_to(jnp.eye(transform.shape[-1], dtype=jnp.float32), transform.shape),
        jnp.zeros_like(shift_term),
    )
    incoming = prefix((transform, shift_term), "ctx", compose, identity_pair, False)[1]
    (outputs, leaving), second_pull = jax.vjp(jax.vmap(section_two), parts, incoming)
    part_grads, local_term = second_pull((cotangent.astype(jnp.float32), jnp.zeros_like(leaving)))
    flipped = jnp.swapaxes(transform, -1, -2)
    departing = prefix((flipped, local_term), "ctx", compose, identity_pair, True)[1]
    more_grads, unused_grad = second_pull((jnp.zeros_like(outputs), departing))
    total_parts = jax.tree.map(jnp.add, part_grads, more_grads)
    grad_mix, grad_weight, grad_decay, grad_rate = first_pull(total_parts)
    returned = from_behind(grad_mix[:, :margin, :].astype(jnp.bfloat16), "ctx", -1).astype(
        jnp.float32
    )
    own_grad = grad_mix[:, margin:, :]
    own_grad = jnp.concatenate(
        [own_grad[:, :-margin, :], own_grad[:, -margin:, :] + returned], axis=1
    )
    total_conv = lax.psum(grad_weight, ("dp", "ctx"))
    tokens_all = mixed.shape[0] * lax.axis_size("dp") * mixed.shape[1] * lax.axis_size("ctx")
    return (
        outputs.astype(jnp.bfloat16),
        own_grad.astype(jnp.bfloat16),
        grad_decay,
        grad_rate,
        total_conv / math.sqrt(tokens_all),
    )


def tree_sum(value, axis):
    count = lax.axis_size(axis)
    if count & (count - 1):
        return lax.psum(value, axis)
    step = 1
    while step < count:
        value = value + lax.ppermute(value, axis, [(i, i ^ step) for i in range(count)])
        step = step * 2
    return value


def prepare_heads(mix_ext, seg_ext, conv_weight, key_heads, value_heads):
    margin = conv_weight.shape[0] - 1
    positions = mix_ext.shape[0] - margin
    current = seg_ext[margin:]
    summed = jnp.zeros((positions, mix_ext.shape[1]), jnp.float32)
    for tap_index in range(margin + 1):
        same_doc = (seg_ext[tap_index : tap_index + positions] == current).astype(jnp.float32)
        summed = (
            summed
            + conv_weight[tap_index][None, :]
            * mix_ext[tap_index : tap_index + positions]
            * same_doc[:, None]
        )
    activated = jax.nn.silu(summed)
    split_at = key_heads * DK
    queries = activated[:, :split_at].reshape(positions, key_heads, DK)
    keyset = activated[:, split_at : 2 * split_at].reshape(positions, key_heads, DK)
    values = activated[:, 2 * split_at :].reshape(positions, value_heads, DV)
    queries = (
        queries
        / jnp.sqrt(jnp.sum(queries * queries, axis=-1, keepdims=True) + 1e-06)
        / math.sqrt(DK)
    )
    keyset = keyset / jnp.sqrt(jnp.sum(keyset * keyset, axis=-1, keepdims=True) + 1e-06)
    repeats = value_heads // key_heads
    return (jnp.repeat(queries, repeats, axis=1), jnp.repeat(keyset, repeats, axis=1), values)


def combine_maps(earlier, later):
    merged = jnp.einsum("...ij,...jk->...ik", later[0], earlier[0], precision=HIGHEST)
    moved = jnp.einsum("...ij,...jk->...ik", later[0], earlier[1], precision=HIGHEST) + later[1]
    return (merged, moved)


def inclusive_states(transform, shift_term):
    blocks = transform.shape[0]
    reach = 1
    while reach < blocks:
        moved = jnp.einsum(
            "bhij,bhjk->bhik", transform[reach:], shift_term[:-reach], precision=HIGHEST
        )
        shift_term = jnp.concatenate([shift_term[:reach], shift_term[reach:] + moved], axis=0)
        if 2 * reach < blocks:
            merged = jnp.einsum(
                "bhij,bhjk->bhik", transform[reach:], transform[:-reach], precision=HIGHEST
            )
            transform = jnp.concatenate([transform[:reach], merged], axis=0)
        reach = reach * 2
    return shift_term


@jax.custom_vjp
def entering_states(transform, shift_term):
    return entering_forward(transform, shift_term)[0]


def entering_forward(transform, shift_term):
    eye = jnp.broadcast_to(jnp.eye(transform.shape[-1], dtype=transform.dtype), transform[:1].shape)
    shifted_maps = jnp.concatenate([eye, transform[:-1]], axis=0)
    shifted_terms = jnp.concatenate([jnp.zeros_like(shift_term[:1]), shift_term[:-1]], axis=0)
    states = inclusive_states(shifted_maps, shifted_terms)
    return states, (transform, states)


def entering_backward(saved, grad_states):
    transform, states = saved
    flipped = jnp.swapaxes(transform, -1, -2)[::-1]
    total = inclusive_states(flipped, grad_states[::-1])[::-1]
    later = total[1:]
    grad_shift = jnp.concatenate([later, jnp.zeros_like(later[:1])], axis=0)
    grad_map = jnp.einsum("bhik,bhjk->bhij", later, states[:-1], precision=HIGHEST)
    grad_transform = jnp.concatenate([grad_map, jnp.zeros_like(transform[:1])], axis=0)
    return (grad_transform, grad_shift)


entering_states.defvjp(entering_forward, entering_backward)


def heads_forward(mix_in, weight_in, decay_in, rate_in, seg_ext, key_heads, value_heads):
    margin = weight_in.shape[0] - 1
    positions = decay_in.shape[0]
    blocks = positions // BLOCK
    mix_ext = jnp.concatenate([jnp.zeros((margin, mix_in.shape[1]), jnp.float32), mix_in], axis=0)
    queries, keyset, values = prepare_heads(mix_ext, seg_ext, weight_in, key_heads, value_heads)
    segments = seg_ext[margin:]
    before = seg_ext[margin - 1 : margin - 1 + positions : BLOCK]

    def blocked(tensor):
        return tensor.reshape((blocks, BLOCK) + tensor.shape[1:])

    parts = jax.vmap(block_parts)(
        blocked(queries),
        blocked(keyset),
        blocked(values),
        blocked(decay_in),
        blocked(rate_in),
        blocked(segments),
        before,
    )
    transform, shift_term = jax.vmap(block_map)(parts)
    incoming = entering_states(transform, shift_term)
    outputs, unused = jax.vmap(block_apply)(parts, incoming)
    return outputs.transpose(0, 2, 1, 3).reshape(positions, value_heads * DV)


def heads_local(mixed, conv_weight, log_decay, write_rate, segment_ids, cotangent):
    if mixed.shape[0] != 1:
        return local(mixed, conv_weight, log_decay, write_rate, segment_ids, cotangent)
    count = lax.axis_size("ctx")
    mine = lax.axis_index("ctx")
    value_heads = HV // count
    key_heads = value_heads * HK // HV
    margin = conv_weight.shape[0] - 1
    rows = mixed.shape[1]
    length = rows * count
    qk_width = key_heads * DK
    v_width = value_heads * DV

    def to_heads(array, width):
        grouped = array.reshape(rows, count, width)
        return lax.all_to_all(grouped, "ctx", 1, 0, tiled=True).reshape(length, width)

    def to_rows(array, width):
        grouped = array.reshape(count, rows, 1, width)
        return lax.all_to_all(grouped, "ctx", 0, 2, tiled=True).reshape(rows, count, width)

    own = mixed[0]
    packed = jnp.concatenate(
        [
            own[:, : HK * DK].reshape(rows, count, qk_width),
            own[:, HK * DK : 2 * HK * DK].reshape(rows, count, qk_width),
            own[:, 2 * HK * DK :].reshape(rows, count, v_width),
        ],
        axis=-1,
    )
    width = 2 * qk_width + v_width
    mix_heads = to_heads(packed, width).astype(jnp.float32)
    decay_heads = to_heads(log_decay[0], value_heads)
    rate_heads = to_heads(write_rate[0], value_heads)
    cot_heads = to_heads(cotangent[0], v_width).astype(jnp.float32)
    segments = lax.all_gather(segment_ids[0], "ctx", tiled=True)
    seg_ext = jnp.concatenate([jnp.full((margin,), -1, jnp.int32), segments.astype(jnp.int32)])

    weight_q = conv_weight[:, : HK * DK].reshape(-1, count, qk_width)[:, mine]
    weight_k = conv_weight[:, HK * DK : 2 * HK * DK].reshape(-1, count, qk_width)[:, mine]
    weight_v = conv_weight[:, 2 * HK * DK :].reshape(-1, count, v_width)[:, mine]
    weight_heads = jnp.concatenate([weight_q, weight_k, weight_v], axis=-1)

    def forward(mix_in, weight_in, decay_in, rate_in):
        return heads_forward(
            mix_in, weight_in, decay_in, rate_in, seg_ext, key_heads, value_heads
        )

    outputs, pullback = jax.vjp(forward, mix_heads, weight_heads, decay_heads, rate_heads)
    grad_mix, grad_weight, grad_decay, grad_rate = pullback(cot_heads)

    core = to_rows(outputs.astype(jnp.bfloat16), v_width).reshape(1, rows, HV * DV)
    back = to_rows(grad_mix.astype(jnp.bfloat16), width)
    grad_rows = jnp.concatenate(
        [
            back[:, :, :qk_width].reshape(rows, HK * DK),
            back[:, :, qk_width : 2 * qk_width].reshape(rows, HK * DK),
            back[:, :, 2 * qk_width :].reshape(rows, HV * DV),
        ],
        axis=-1,
    )[None]
    decay_rows = to_rows(grad_decay, value_heads).reshape(1, rows, HV)
    rate_rows = to_rows(grad_rate, value_heads).reshape(1, rows, HV)

    taps = conv_weight.shape[0]

    def place(part, total_width, part_width):
        slots = jnp.zeros((taps, count, part_width), jnp.float32)
        slots = lax.dynamic_update_slice(slots, part[:, None, :], (0, mine, 0))
        return slots.reshape(taps, total_width)

    placed = jnp.concatenate(
        [
            place(grad_weight[:, :qk_width], HK * DK, qk_width),
            place(grad_weight[:, qk_width : 2 * qk_width], HK * DK, qk_width),
            place(grad_weight[:, 2 * qk_width :], HV * DV, v_width),
        ],
        axis=-1,
    )
    total_conv = tree_sum(tree_sum(placed, "ctx"), "dp")
    tokens_all = mixed.shape[0] * lax.axis_size("dp") * length
    return (core, grad_rows, decay_rows, rate_rows, total_conv / math.sqrt(tokens_all))


def solution(mesh):
    in_specs = (
        P("dp", "ctx", None),
        P(),
        P("dp", "ctx", None),
        P("dp", "ctx", None),
        P("dp", "ctx"),
        P("dp", "ctx", None),
    )
    out_specs = (
        P("dp", "ctx", None),
        P("dp", "ctx", None),
        P("dp", "ctx", None),
        P("dp", "ctx", None),
        P(),
    )
    count = mesh.shape["ctx"]
    per_device = HV // count if HV % count == 0 else 0
    chosen = heads_local if per_device and (per_device * HK) % HV == 0 else local
    return jax.shard_map(chosen, mesh=mesh, in_specs=in_specs, out_specs=out_specs, check_vma=False)
```

profile of v0, /device:TPU:0, one launch (start us, length us, event | category | flops | bytes accessed | tf_op | source)
XLA Modules:
  0.0 353.4 jit_solution(9149305256029222995)
XLA Ops:
  0.6 5.2 %all-to-all-start.1 = ((f32[128,8,2]{0,2,1:T(2,128)}), f32[128,8,2]{0,2,1:T(2,128)S(1)}, u32[]{:S(2)}, u32[]{:S(2)}) async-start(f32[128,8,2]{0,2,1:T(2,128)} %bitcast.354), calls=%async_computation.1 | async-start | bytes 16384 | tf_op jit(solution)/shard_map/all_to_all | solution.py:374
  9.0 9.3 %all-gather = s32[1,1024]{1,0:T(1,128)S(1)} all-gather(s32[1,128]{1,0:T(1,128)S(1)} %copy-done.140), channel_id=2, replica_groups=mesh['dp'=4,'ctx'=8] {'ctx'}, dimensions={1}, use_global_device_ids=true | all-gather | bytes 4608 | tf_op jit(solution)/shard_map/all_gather | solution.py:394
  25.8 3.6 %all-to-all-done.2 = f32[128,8,2]{0,2,1:T(2,128)S(1)} async-done(((f32[128,8,2]{0,2,1:T(2,128)}), f32[128,8,2]{0,2,1:T(2,128)S(1)}, u32[]{:S(2)}, u32[]{:S(2)}) %all-to-all-start.2) | async-done | bytes 8224 | tf_op jit(solution)/shard_map/all_to_all | solution.py:374
  29.4 3.5 all-to-all-start.4
  34.3 8.2 %all-to-all-done.4 = bf16[128,8,256]{2,0,1:T(8,128)(2,1)S(1)} async-done(((bf16[128,8,256]{2,0,1:T(8,128)(2,1)}), bf16[128,8,256]{2,0,1:T(8,128)(2,1)S(1)}, u32[]{:S(2)}, u32[]{:S(2)}) %all-to-all-start.4) | async-done | bytes 524320 | tf_op jit(solution)/shard_map/all_to_all | solution.py:374
  42.5 3.6 %all-to-all-start = ((bf16[128,8,512]{0,2,1:T(8,128)(2,1)}), bf16[128,8,512]{0,2,1:T(8,128)(2,1)S(1)}, u32[]{:S(2)}, u32[]{:S(2)}) async-start(bf16[128,8,512]{0,2,1:T(8,128)(2,1)} %pad_maximum_fusion.19), calls=%async_computation | async-start | bytes 2097152 | tf_op jit(solution)/shard_map/all_to_all | solution.py:374
  46.1 6.3 %fusion.269 = f32[16,64,2]{2,0,1:T(8,128)S(1)} fusion(f32[16,64,2]{2,0,1:T(8,128)S(1)} %copy.455), kind=kOutput, calls=%fused_computation.386 | output fusion | flops 129024 | bytes 16384 | tf_op jit(solution)/shard_map/jvp(vmap(jit(cumsum)))/reduce_window_sum | solution.py:84
  113.9 4.9 %fusion.6 = f32[15,2,128,128]{3,2,1,0:T(8,128)} fusion(f32[16,2,64,256]{3,2,1,0:T(8,128)S(1)} %fusion.39, f32[16,2,64]{2,1,0:T(2,128)S(1)} %copy-done.88, f32[16,64,128]{2,1,0:T(8,128)S(1)} %bitcast.287), kind=kOutput, calls=%fused_computation.7 | convolution fusion | flops 377749504 | bytes 3555328 | tf_op jit(solution)/shard_map/jvp()/slice | solution.py:313
  118.7 5.3 %fusion.4 = f32[16,2,128,128]{3,2,1,0:T(8,128)} fusion(f32[16,2,64,256]{3,2,1,0:T(8,128)S(1)} %fusion.39, f32[16,2,64]{2,1,0:T(2,128)S(1)} %copy-done.88, f32[16,64,128]{2,1,0:T(8,128)S(1)} %bitcast.288), kind=kOutput, calls=%fused_computation.5 | convolution fusion | flops 402915328 | bytes 3686400 | tf_op jit(solution)/shard_map/jvp(vmap(hcd,hce->hde))/dot_general | solution.py:117
  131.3 3.4 fusion.58
  151.9 3.9 %multiply_reduce_fusion.8 = (f32[16,64,2]{1,2,0:T(2,128)}, f32[16,64,2,128]{3,1,2,0:T(8,128)}) fusion(f32[16,64,128]{2,1,0:T(8,128)S(1)} %bitcast.299, bf16[16,64,2,128]{3,2,1,0:T(2,128)(2,1)S(1)} %copy-done.66, f32[8,2,128,128]{3,2,1,0:T(8,128)S(1)} %convolution_add_fusion.11, f32[8,2,128,128]{3,2,1,0:T(8,128)S(1)} %pad_maximum_fusion.17), kind=kOutput, calls=%fused_computation.163 | convolution fusion | flops 403699712 | bytes 4202496 | tf_op jit(solution)/shard_map/transpose(jvp(vmap(hcd,hde->hce)))/dot_general | solution.py:129
  158.9 3.6 %convolution_add_fusion = f32[16,2,128,128]{3,2,1,0:T(8,128)S(1)} fusion(f32[16,2,128,128]{3,2,1,0:T(8,128)S(1)} %fusion.54, f32[16,2,64,128]{3,2,1,0:T(8,128)S(1)} %fusion.137, f32[16,2,64,256]{3,2,1,0:T(8,128)S(1)} %copy-done.20), kind=kOutput, calls=%fused_computation.77 | convolution fusion | flops 403439616 | bytes 6291456 | tf_op jit(solution)/shard_map/transpose(jvp(vmap(hcd,hde->hce)))/dot_general | solution.py:126
  171.2 5.6 %reverse_add_fusion = f32[15,2,128,128]{3,2,1,0:T(8,128)S(1)} fusion(f32[15,2,128,128]{3,2,1,0:T(8,128)} %slice.341, f32[15,2,128,128]{2,3,1,0:T(8,128)S(1)} %slice.290, f32[16,2,128,128]{3,2,1,0:T(8,128)} %copy-done.24), kind=kOutput, calls=%fused_computation.61 | convolution fusion | flops 755466240 | bytes 7864320 | tf_op jit(solution)/shard_map/transpose(jvp(bhij,bhjk->bhik))/dot_general | solution.py:354
  176.8 4.9 %fusion.21 = f32[15,2,128,128]{3,2,1,0:T(8,128)S(1)} fusion(f32[15,2,128,128]{2,3,1,0:T(8,128)} %copy-done, f32[15,2,128,128]{2,3,1,0:T(8,128)S(1)} %copy-done.69), kind=kOutput, calls=%fused_computation.54 | convolution fusion | flops 754974720 | bytes 5898240 | tf_op jit(solution)/shard_map/transpose(jvp(bhij,bhjk->bhik))/dot_general | solution.py:354
  199.8 5.3 %fusion.13 = f32[16,2,64,128]{3,2,1,0:T(8,128)S(1)} fusion(f32[15,2,128,128]{3,2,1,0:T(8,128)S(1)} %slice.311, f32[16,2,64,256]{3,2,1,0:T(8,128)} %copy-done.19), kind=kOutput, calls=%fused_computation.38 | convolution fusion | flops 402653184 | bytes 4063232 | tf_op jit(solution)/shard_map/transpose(jvp(vmap(hcd,hce->hde)))/dot_general | solution.py:120
  205.2 3.7 %fusion.68 = f32[16,2,64,128]{3,2,1,0:T(8,128)S(1)} fusion(f32[16,2,64,128]{3,2,1,0:T(8,128)S(1)} %copy-done.58, f32[15,2,128,128]{3,2,1,0:T(8,128)} %copy-done.12, f32[16,2,64]{2,1,0:T(2,128)S(1)} %copy-done.89, f32[16,64,128]{2,1,0:T(8,128)S(1)} %bitcast.290), kind=kOutput, calls=%fused_computation.108 | convolution fusion | flops 403177472 | bytes 4595712 | tf_op jit(solution)/shard_map/transpose(jvp(vmap(hcd,hce->hde)))/dot_general | solution.py:120
  208.9 4.6 %fusion.17 = f32[15,2,128,128]{2,3,1,0:T(8,128)S(1)} fusion(f32[15,2,128,128]{3,2,1,0:T(8,128)S(1)} %copy-done.13, f32[8,2,128,128]{3,2,1,0:T(8,128)S(1)} %copy-done.9, f32[8,2,128,128]{3,2,1,0:T(8,128)S(1)} %pad_maximum_fusion.17), kind=kOutput, calls=%fused_computation.49 | convolution fusion | flops 755466240 | bytes 6029312 | tf_op jit(solution)/shard_map/transpose(jvp(bhik,bhjk->bhij))/dot_general | solution.py:354
  213.5 4.1 %fusion.105 = f32[16,2,64,128]{3,2,1,0:T(8,128)S(1)} fusion(f32[16,2,64,128]{3,2,1,0:T(8,128)S(1)} %copy-done.58, f32[8,2,128,128]{3,2,1,0:T(8,128)S(1)} %copy-done.9, f32[8,2,128,128]{3,2,1,0:T(8,128)S(1)} %pad_maximum_fusion.17), kind=kOutput, calls=%fused_computation.170 | convolution fusion | flops 403439616 | bytes 4194304 | tf_op jit(solution)/shard_map/transpose(jvp(vmap(hcd,hde->hce)))/dot_general | solution.py:126
  217.9 4.1 %fusion.73 = f32[16,2,64,128]{3,2,1,0:T(8,128)S(1)} fusion(f32[16,2,64,128]{3,2,1,0:T(8,128)S(1)} %fusion.105, f32[15,2,128,128]{2,3,1,0:T(8,128)S(1)} %fusion.17, f32[16,2,64]{2,1,0:T(2,128)S(1)} %copy-done.89, f32[16,64,128]{2,1,0:T(8,128)S(1)} %bitcast.291), kind=kOutput, calls=%fused_computation.109 | convolution fusion | flops 403701760 | bytes 4595712 | tf_op jit(solution)/shard_map/transpose(jvp(vmap(hcd,hce->hde)))/dot_general | solution.py:117
  300.1 4.7 %fusion.139 = f32[16,2,64,128]{3,2,1,0:T(8,128)} fusion(f32[16,2,64,128]{3,2,1,0:T(8,128)} %convolution_subtract_fusion, f32[16,2,64,64]{2,3,1,0:T(8,128)} %copy-done.33, f32[16,2,64]{2,1,0:T(2,128)S(1)} %copy.462, pred[16,64,64]{1,2,0:T(8,128)(4,1)S(1)} %copy-done.75), kind=kOutput, calls=%fused_computation.205 | convolution fusion | flops 201850880 | bytes 2695168 | tf_op jit(solution)/shard_map/jvp(vmap(hij,hje->hie))/dot_general | solution.py:130
  317.1 4.1 %all-to-all-start.3 = ((bf16[8,128,1,256]{3,1,2,0:T(8,128)(2,1)}), bf16[8,128,1,256]{3,1,2,0:T(8,128)(2,1)S(1)}, u32[]{:S(2)}, u32[]{:S(2)}) async-start(bf16[8,128,1,256]{3,1,2,0:T(8,128)(2,1)} %bitcast.28), calls=%async_computation.3 | async-start | bytes 1048576 | tf_op jit(solution)/shard_map/all_to_all | solution.py:378
  326.9 4.0 %all-to-all-done.3 = bf16[8,128,1,256]{3,1,2,0:T(8,128)(2,1)S(1)} async-done(((bf16[8,128,1,256]{3,1,2,0:T(8,128)(2,1)}), bf16[8,128,1,256]{3,1,2,0:T(8,128)(2,1)S(1)}, u32[]{:S(2)}, u32[]{:S(2)}) %all-to-all-start.3) | async-done | bytes 524320 | tf_op jit(solution)/shard_map/all_to_all | solution.py:378
  330.9 3.6 %all-to-all-start.5 = ((bf16[8,128,1,512]{3,1,2,0:T(8,128)(2,1)}), bf16[8,128,1,512]{3,1,2,0:T(8,128)(2,1)S(1)}, u32[]{:S(2)}, u32[]{:S(2)}) async-start(bf16[8,128,1,512]{3,1,2,0:T(8,128)(2,1)} %bitcast.47), calls=%async_computation.5 | async-start | bytes 2097152 | tf_op jit(solution)/shard_map/all_to_all | solution.py:378
  336.5 13.4 %all-to-all-done.5 = bf16[8,128,1,512]{3,1,2,0:T(8,128)(2,1)S(1)} async-done(((bf16[8,128,1,512]{3,1,2,0:T(8,128)(2,1)}), bf16[8,128,1,512]{3,1,2,0:T(8,128)(2,1)S(1)}, u32[]{:S(2)}, u32[]{:S(2)}) %all-to-all-start.5) | async-done | bytes 1048608 | tf_op jit(solution)/shard_map/all_to_all | solution.py:378
  (495 shorter events, 227.3 us)
Async XLA Ops:
  0.6 20.7 %all-to-all-start.1 = ((f32[128,8,2]{0,2,1:T(2,128)}), f32[128,8,2]{0,2,1:T(2,128)S(1)}, u32[]{:S(2)}, u32[]{:S(2)}) async-start(f32[128,8,2]{0,2,1:T(2,128)} %bitcast.354), calls=%async_computation.1 | async-start | bytes 16384 | tf_op jit(solution)/shard_map/all_to_all | solution.py:374
  8.3 99.4 %copy-start.70 = (f32[64,64]{0,1:T(8,128)}, f32[64,64]{0,1:T(8,128)S(1)}, u32[]{:S(2)}) copy-start(f32[64,64]{0,1:T(8,128)S(1)} %fusion.208) | copy-start | bytes 49156
  9.0 125.7 %copy-start.76 = (f32[128,128]{0,1:T(8,128)}, f32[128,128]{0,1:T(8,128)S(1)}, u32[]{:S(2)}) copy-start(f32[128,128]{0,1:T(8,128)S(1)} %get-tuple-element.92) | copy-start | bytes 196612
  18.4 46.4 %copy-start.106 = (f32[1024]{0:T(1024)}, f32[1024]{0:T(1024)S(1)}, u32[]{:S(2)}) copy-start(f32[1024]{0:T(1024)S(1)} %get-tuple-element.81) | copy-start | bytes 12292
  18.4 46.4 %copy-start.109 = (f32[1024]{0:T(1024)}, f32[1024]{0:T(1024)S(1)}, u32[]{:S(2)}) copy-start(f32[1024]{0:T(1024)S(1)} %get-tuple-element.82) | copy-start | bytes 12292
  18.4 46.4 %copy-start.112 = (f32[1024]{0:T(1024)}, f32[1024]{0:T(1024)S(1)}, u32[]{:S(2)}) copy-start(f32[1024]{0:T(1024)S(1)} %get-tuple-element.83) | copy-start | bytes 12292
  20.1 34.4 %copy-start.102 = (f32[16,64]{1,0:T(8,128)}, f32[16,64]{1,0:T(8,128)S(1)}, u32[]{:S(2)}) copy-start(f32[16,64]{1,0:T(8,128)S(1)} %get-tuple-element.71) | copy-start | bytes 12292
  20.3 34.9 %copy-start.138 = (f32[16]{0:T(128)}, f32[16]{0:T(128)S(1)}, u32[]{:S(2)}) copy-start(f32[16]{0:T(128)S(1)} %slice_reduce_fusion.1) | copy-start | bytes 196
  21.4 8.0 %all-to-all-start.2 = ((f32[128,8,2]{0,2,1:T(2,128)}), f32[128,8,2]{0,2,1:T(2,128)S(1)}, u32[]{:S(2)}, u32[]{:S(2)}) async-start(f32[128,8,2]{0,2,1:T(2,128)} %bitcast.20), calls=%async_computation.2 | async-start | bytes 16384 | tf_op jit(solution)/shard_map/all_to_all | solution.py:374
  29.4 13.2 %all-to-all-start.4 = ((bf16[128,8,256]{2,0,1:T(8,128)(2,1)}), bf16[128,8,256]{2,0,1:T(8,128)(2,1)S(1)}, u32[]{:S(2)}, u32[]{:S(2)}) async-start(bf16[128,8,256]{2,0,1:T(8,128)(2,1)} %copy.492), calls=%async_computation.4 | async-start | bytes 1048576 | tf_op jit(solution)/shard_map/all_to_all | solution.py:374
  33.9 60.0 %copy-start.61 = (pred[16,64,64]{1,2,0:T(8,128)(4,1)}, pred[16,64,64]{1,2,0:T(8,128)(4,1)S(1)}, u32[]{:S(2)}) copy-start(pred[16,64,64]{1,2,0:T(8,128)(4,1)S(1)} %get-tuple-element.70) | copy-start | bytes 196612
  33.9 124.0 %copy-start.74 = (pred[16,64,64]{1,2,0:T(8,128)(4,1)}, pred[16,64,64]{1,2,0:T(8,128)(4,1)S(1)}, u32[]{:S(2)}) copy-start(pred[16,64,64]{1,2,0:T(8,128)(4,1)S(1)} %get-tuple-element.69) | copy-start | bytes 196612
  42.5 18.9 %all-to-all-start = ((bf16[128,8,512]{0,2,1:T(8,128)(2,1)}), bf16[128,8,512]{0,2,1:T(8,128)(2,1)S(1)}, u32[]{:S(2)}, u32[]{:S(2)}) async-start(bf16[128,8,512]{0,2,1:T(8,128)(2,1)} %pad_maximum_fusion.19), calls=%async_computation | async-start | bytes 2097152 | tf_op jit(solution)/shard_map/all_to_all | solution.py:374
  53.7 40.2 %copy-start.80 = (f32[16,2,64]{2,1,0:T(2,128)}, f32[16,2,64]{2,1,0:T(2,128)S(1)}, u32[]{:S(2)}) copy-start(f32[16,2,64]{2,1,0:T(2,128)S(1)} %copy.461) | copy-start | bytes 24580
  69.8 86.0 %copy-start.22 = (f32[1024,128]{1,0:T(8,128)}, f32[1024,128]{1,0:T(8,128)S(1)}, u32[]{:S(2)}) copy-start(f32[1024,128]{1,0:T(8,128)S(1)} %get-tuple-element.52) | copy-start | bytes 1572868
  291.0 7.1 %collective-permute-start = (f32[4,4096]{1,0:T(4,128)S(1)}, f32[4,4096]{1,0:T(4,128)S(1)}, u32[]{:S(2)}, u32[]{:S(2)}) collective-permute-start(f32[4,4096]{1,0:T(4,128)S(1)} %constant_dynamic-update-slice_fusion), channel_id=1, source_target_pairs={{0,1},{1,0},{2,3},{3,2},{4,5},{5,4},{6,7},{7,6},{8,9},{9,8},{10,11... | collective-permute-start | bytes 196616 | tf_op jit(solution)/shard_map/ppermute | solution.py:249
  294.7 12.3 %all-to-all-start.6 = ((f32[8,128,1,2]{1,3,2,0:T(2,128)}), f32[8,128,1,2]{1,3,2,0:T(2,128)S(1)}, u32[]{:S(2)}, u32[]{:S(2)}) async-start(f32[8,128,1,2]{1,3,2,0:T(2,128)} %copy.541), calls=%async_computation.6 | async-start | bytes 16384 | tf_op jit(solution)/shard_map/all_to_all | solution.py:378
  298.1 7.3 %collective-permute-start.1 = (f32[4,4096]{1,0:T(4,128)S(1)}, f32[4,4096]{1,0:T(4,128)S(1)}, u32[]{:S(2)}, u32[]{:S(2)}) collective-permute-start(f32[4,4096]{1,0:T(4,128)S(1)} %add.184), channel_id=1, source_target_pairs={{0,2},{1,3},{2,0},{3,1},{4,6},{5,7},{6,4},{7,5},{8,10},{9,11},{10,... | collective-permute-start | bytes 196616 | tf_op jit(solution)/shard_map/ppermute | solution.py:249
  305.5 10.0 %collective-permute-start.2 = (f32[4,4096]{1,0:T(4,128)S(1)}, f32[4,4096]{1,0:T(4,128)S(1)}, u32[]{:S(2)}, u32[]{:S(2)}) collective-permute-start(f32[4,4096]{1,0:T(4,128)S(1)} %add.185), channel_id=1, source_target_pairs={{0,4},{1,5},{2,6},{3,7},{4,0},{5,1},{6,2},{7,3},{8,12},{9,13},{10,... | collective-permute-start | bytes 196616 | tf_op jit(solution)/shard_map/ppermute | solution.py:249
  307.0 10.1 %all-to-all-start.7 = ((f32[8,128,1,2]{1,3,2,0:T(2,128)}), f32[8,128,1,2]{1,3,2,0:T(2,128)S(1)}, u32[]{:S(2)}, u32[]{:S(2)}) async-start(f32[8,128,1,2]{1,3,2,0:T(2,128)} %copy.546), calls=%async_computation.7 | async-start | bytes 16384 | tf_op jit(solution)/shard_map/all_to_all | solution.py:378
  315.5 6.7 %collective-permute-start.3 = (f32[4,4096]{1,0:T(4,128)S(1)}, f32[4,4096]{1,0:T(4,128)S(1)}, u32[]{:S(2)}, u32[]{:S(2)}) collective-permute-start(f32[4,4096]{1,0:T(4,128)S(1)} %add.186), channel_id=1, source_target_pairs={{0,8},{8,0},{16,24},{24,16},{1,9},{9,1},{17,25},{25,17},{2,10},{10... | collective-permute-start | bytes 196616 | tf_op jit(solution)/shard_map/ppermute | solution.py:249
  317.1 13.8 %all-to-all-start.3 = ((bf16[8,128,1,256]{3,1,2,0:T(8,128)(2,1)}), bf16[8,128,1,256]{3,1,2,0:T(8,128)(2,1)S(1)}, u32[]{:S(2)}, u32[]{:S(2)}) async-start(bf16[8,128,1,256]{3,1,2,0:T(8,128)(2,1)} %bitcast.28), calls=%async_computation.3 | async-start | bytes 1048576 | tf_op jit(solution)/shard_map/all_to_all | solution.py:378
  322.2 12.3 %collective-permute-start.4 = (f32[4,4096]{1,0:T(4,128)S(1)}, f32[4,4096]{1,0:T(4,128)S(1)}, u32[]{:S(2)}, u32[]{:S(2)}) collective-permute-start(f32[4,4096]{1,0:T(4,128)S(1)} %add.187), channel_id=1, source_target_pairs={{0,16},{8,24},{16,0},{24,8},{1,17},{9,25},{17,1},{25,9},{2,18},{10... | collective-permute-start | bytes 196616 | tf_op jit(solution)/shard_map/ppermute | solution.py:249
  330.9 18.9 %all-to-all-start.5 = ((bf16[8,128,1,512]{3,1,2,0:T(8,128)(2,1)}), bf16[8,128,1,512]{3,1,2,0:T(8,128)(2,1)S(1)}, u32[]{:S(2)}, u32[]{:S(2)}) async-start(bf16[8,128,1,512]{3,1,2,0:T(8,128)(2,1)} %bitcast.47), calls=%async_computation.5 | async-start | bytes 2097152 | tf_op jit(solution)/shard_map/all_to_all | solution.py:378
  (132 other events, 648.6 us)
where the time goes:
time: 361 us; the launch traced here: 353 us
  matrix products  178 us (49%)
  local copies, waits for them, and re-layouts  58 us (16%)
  starting transfers between devices  37.9 us (10%)
  other arithmetic  34.5 us (10%)
  waiting for transfers between devices  32.6 us (9%)
  blocking collectives  9.31 us (3%)
    dot_general x15, matrix products, unit_lower_inverse(): power = jnp.einsum('hij,hjk->hik', power, power, precision=HIGHEST)  33.7 us
    dot_general x15, matrix products, unit_lower_inverse(): jnp.einsum('hij,hjk->hik', result, identity_matrix + power, precision=HIG...  32.7 us
    dot_general x7, matrix products, heads_forward(): incoming = entering_states(transform, shift_term)  23.2 us
    all_to_all x4, waiting for transfers between devices, to_rows(): lax.all_to_all(grouped, 'ctx', 0, 2, tiled=True).reshape(rows, count, width)  17.4 us
    unnamed x299, local copies, waits for them, and re-layouts  16.5 us
    all_to_all x4, starting transfers between devices, to_heads(): lax.all_to_all(grouped, 'ctx', 1, 0, tiled=True).reshape(length, width)  15.6 us
    all_to_all x4, waiting for transfers between devices, to_heads(): lax.all_to_all(grouped, 'ctx', 1, 0, tiled=True).reshape(length, width)  15.2 us
    all_to_all x4, starting transfers between devices, to_rows(): lax.all_to_all(grouped, 'ctx', 0, 2, tiled=True).reshape(rows, count, width)  14.3 us
  transfers between devices with their start and end apart: 13, of which 5 were waited for; matrix products, arithmetic and copies ran while one was open for 11% of the time, Pallas kernels for 0%

commit v1 on v0

--- a/solution.py
+++ b/solution.py
@@ -378,21 +378,35 @@
         return lax.all_to_all(grouped, "ctx", 0, 2, tiled=True).reshape(rows, count, width)
 
     own = mixed[0]
+    width = 2 * qk_width + v_width
     packed = jnp.concatenate(
         [
             own[:, : HK * DK].reshape(rows, count, qk_width),
             own[:, HK * DK : 2 * HK * DK].reshape(rows, count, qk_width),
             own[:, 2 * HK * DK :].reshape(rows, count, v_width),
+            cotangent[0].reshape(rows, count, v_width),
         ],
         axis=-1,
     )
-    width = 2 * qk_width + v_width
-    mix_heads = to_heads(packed, width).astype(jnp.float32)
-    decay_heads = to_heads(log_decay[0], value_heads)
-    rate_heads = to_heads(write_rate[0], value_heads)
-    cot_heads = to_heads(cotangent[0], v_width).astype(jnp.float32)
-    segments = lax.all_gather(segment_ids[0], "ctx", tiled=True)
-    seg_ext = jnp.concatenate([jnp.full((margin,), -1, jnp.int32), segments.astype(jnp.int32)])
+    wide = to_heads(packed, width + v_width)
+    mix_heads = wide[:, :width].astype(jnp.float32)
+    cot_heads = wide[:, width:].astype(jnp.float32)
+    seg_columns = jnp.broadcast_to(
+        segment_ids[0].astype(jnp.float32)[:, None, None], (rows, count, 1)
+    )
+    small = jnp.concatenate(
+        [
+            log_decay[0].reshape(rows, count, value_heads),
+            write_rate[0].reshape(rows, count, value_heads),
+            seg_columns,
+        ],
+        axis=-1,
+    )
+    narrow = to_heads(small, 2 * value_heads + 1)
+    decay_heads = narrow[:, :value_heads]
+    rate_heads = narrow[:, value_heads : 2 * value_heads]
+    segments = narrow[:, 2 * value_heads].astype(jnp.int32)
+    seg_ext = jnp.concatenate([jnp.full((margin,), -1, jnp.int32), segments])
 
     weight_q = conv_weight[:, : HK * DK].reshape(-1, count, qk_width)[:, mine]
     weight_k = conv_weight[:, HK * DK : 2 * HK * DK].reshape(-1, count, qk_width)[:, mine]
@@ -407,18 +421,20 @@
     outputs, pullback = jax.vjp(forward, mix_heads, weight_heads, decay_heads, rate_heads)
     grad_mix, grad_weight, grad_decay, grad_rate = pullback(cot_heads)
 
-    core = to_rows(outputs.astype(jnp.bfloat16), v_width).reshape(1, rows, HV * DV)
-    back = to_rows(grad_mix.astype(jnp.bfloat16), width)
+    joined = jnp.concatenate([outputs.astype(jnp.bfloat16), grad_mix.astype(jnp.bfloat16)], axis=-1)
+    back = to_rows(joined, v_width + width)
+    core = back[:, :, :v_width].reshape(1, rows, HV * DV)
     grad_rows = jnp.concatenate(
         [
-            back[:, :, :qk_width].reshape(rows, HK * DK),
-            back[:, :, qk_width : 2 * qk_width].reshape(rows, HK * DK),
-            back[:, :, 2 * qk_width :].reshape(rows, HV * DV),
+            back[:, :, v_width : v_width + qk_width].reshape(rows, HK * DK),
+            back[:, :, v_width + qk_width : v_width + 2 * qk_width].reshape(rows, HK * DK),
+            back[:, :, v_width + 2 * qk_width :].reshape(rows, HV * DV),
         ],
         axis=-1,
     )[None]
-    decay_rows = to_rows(grad_decay, value_heads).reshape(1, rows, HV)
-    rate_rows = to_rows(grad_rate, value_heads).reshape(1, rows, HV)
+    grads_small = to_rows(jnp.concatenate([grad_decay, grad_rate], axis=-1), 2 * value_heads)
+    decay_rows = grads_small[:, :, :value_heads].reshape(1, rows, HV)
+    rate_rows = grads_small[:, :, value_heads:].reshape(1, rows, HV)
 
     taps = conv_weight.shape[0]
 

time: 361 us -> 343 us (0.950)
  starting transfers between devices: 37.9 us -> 25 us
  blocking collectives: 9.31 us -> 0 us
    ppermute x5, waiting for transfers between devices: 0.01 us -> 26.6 us  [tree_sum(): lax.ppermute(value, axis, [(i, i ^ step) for i in range(count)])]
    all_to_all x4 -> x2, waiting for transfers between devices: 17.4 us -> 0.01 us  [to_rows(): lax.all_to_all(grouped, 'ctx', 0, 2, tiled=True).reshape(rows, count, width)]
    all_gather x1 -> x0, blocking collectives: 9.31 us -> none  [heads_local(): segments = lax.all_gather(segment_ids[0], 'ctx', tiled=True)]
    all_to_all x4 -> x2, starting transfers between devices: 14.3 us -> 7.45 us  [to_rows(): lax.all_to_all(grouped, 'ctx', 0, 2, tiled=True).reshape(rows, count, width)]
    all_to_all x4 -> x2, waiting for transfers between devices: 15.2 us -> 8.46 us  [to_heads(): lax.all_to_all(grouped, 'ctx', 1, 0, tiled=True).reshape(length, width)]
    all_to_all x4 -> x2, starting transfers between devices: 15.6 us -> 9.4 us  [to_heads(): lax.all_to_all(grouped, 'ctx', 1, 0, tiled=True).reshape(length, width)]
    unnamed x299 -> x300, local copies, waits for them, and re-layouts: 16.5 us -> 19.2 us
  transfers between devices with their start and end apart: 13 -> 9, of which waited for: 5 -> 5; matrix products, arithmetic and copies ran while one was open for 11% -> 9% of each run, Pallas kernels for 0% -> 0%
where the time goes in v1:
time: 343 us; the launch traced here: 337 us
  matrix products  178 us (52%)
  local copies, waits for them, and re-layouts  58.4 us (17%)
  other arithmetic  37.2 us (11%)
  waiting for transfers between devices  35.1 us (10%)
  starting transfers between devices  25 us (7%)
    dot_general x15, matrix products, unit_lower_inverse(): power = jnp.einsum('hij,hjk->hik', power, power, precision=HIGHEST)  33.6 us
    dot_general x15, matrix products, unit_lower_inverse(): jnp.einsum('hij,hjk->hik', result, identity_matrix + power, precision=HIG...  32.6 us
    ppermute x5, waiting for transfers between devices, tree_sum(): lax.ppermute(value, axis, [(i, i ^ step) for i in range(count)])  26.6 us
    dot_general x7, matrix products, heads_forward(): incoming = entering_states(transform, shift_term)  23.2 us
    unnamed x300, local copies, waits for them, and re-layouts  19.2 us
    dot_general x3, matrix products, block_map(): jnp.einsum('hcd,hce->hde', tail_keys, write_keys, precision=HIGHEST)  12.5 us
    dot_general x3, matrix products, block_apply(): jnp.einsum('hcd,hde->hce', write_keys, state_in, precision=HIGHEST)  10.9 us
    dot_general x4, matrix products, inclusive_states(): jnp.einsum('bhij,bhjk->bhik', transform[reach:], shift_term[:-reach], pre...  9.6 us
  transfers between devices with their start and end apart: 9, of which 5 were waited for; matrix products, arithmetic and copies ran while one was open for 9% of the time, Pallas kernels for 0%

profile of v1, /device:TPU:0, one launch (start us, length us, event | category | flops | bytes accessed | tf_op | source)
XLA Modules:
  0.0 336.7 jit_solution(10221136646138111957)
XLA Ops:
  2.6 5.2 %all-to-all-start.1 = ((f32[128,8,5]{0,2,1:T(8,128)}), f32[128,8,5]{0,2,1:T(8,128)S(1)}, u32[]{:S(2)}, u32[]{:S(2)}) async-start(f32[128,8,5]{0,2,1:T(8,128)} %pad_maximum_fusion.25), calls=%async_computation.1 | async-start | bytes 65536 | tf_op jit(solution)/shard_map/all_to_all | solution.py:374
  14.0 4.2 %all-to-all-start = ((bf16[128,8,768]{0,2,1:T(8,128)(2,1)}), bf16[128,8,768]{0,2,1:T(8,128)(2,1)S(1)}, u32[]{:S(2)}, u32[]{:S(2)}) async-start(bf16[128,8,768]{0,2,1:T(8,128)(2,1)} %pad_maximum_fusion.12), calls=%async_computation | async-start | bytes 3145728 | tf_op jit(solution)/shard_map/all_to_all | solution.py:374
  18.6 6.3 %fusion.274 = f32[16,64,2]{2,0,1:T(8,128)S(1)} fusion(f32[16,64,2]{2,0,1:T(8,128)S(1)} %copy.456), kind=kOutput, calls=%fused_computation.396 | output fusion | flops 129024 | bytes 16384 | tf_op jit(solution)/shard_map/jvp(vmap(jit(cumsum)))/reduce_window_sum | solution.py:84
  30.7 8.5 %all-to-all-done = bf16[128,8,768]{0,2,1:T(8,128)(2,1)S(1)} async-done(((bf16[128,8,768]{0,2,1:T(8,128)(2,1)}), bf16[128,8,768]{0,2,1:T(8,128)(2,1)S(1)}, u32[]{:S(2)}, u32[]{:S(2)}) %all-to-all-start) | async-done | bytes 1572896 | tf_op jit(solution)/shard_map/all_to_all | solution.py:374
  69.6 3.3 fusion.121
  88.4 4.9 %fusion.6 = f32[15,2,128,128]{3,2,1,0:T(8,128)} fusion(f32[16,2,64,256]{3,2,1,0:T(8,128)S(1)} %fusion.39, f32[16,2,64]{2,1,0:T(2,128)S(1)} %copy.460, f32[16,64,128]{2,1,0:T(8,128)S(1)} %bitcast.267), kind=kOutput, calls=%fused_computation.7 | convolution fusion | flops 377749504 | bytes 3555328 | tf_op jit(solution)/shard_map/jvp()/slice | solution.py:313
  93.2 5.3 %fusion.4 = f32[16,2,128,128]{3,2,1,0:T(8,128)} fusion(f32[16,2,64,256]{3,2,1,0:T(8,128)S(1)} %fusion.39, f32[16,2,64]{2,1,0:T(2,128)S(1)} %copy.460, f32[16,64,128]{2,1,0:T(8,128)S(1)} %bitcast.268), kind=kOutput, calls=%fused_computation.5 | convolution fusion | flops 402915328 | bytes 3686400 | tf_op jit(solution)/shard_map/jvp(vmap(hcd,hce->hde))/dot_general | solution.py:117
  103.4 4.3 %bitcast_subtract_fusion = (f32[16,2,128,128]{2,3,1,0:T(8,128)}, f32[16,2,128,128]{2,3,1,0:T(8,128)S(1)}) fusion(f32[16,2,128,128]{3,2,1,0:T(8,128)} %fusion.4, f32[128,128]{0,1:T(8,128)S(1)} %copy-done.96, f32[16,2]{1,0:T(8,128)S(1)} %copy-done.125, f32[16,2,128,128]{2,3,1,0:T(8,128)} %copy.482, f32[128,128]{0,1:T(8,128)S(1)} %get-tuple-element.98), kind=kLoop, calls=%fused_computation.24 | loop fusion | flops 2097152 | bytes 8519808 | tf_op jit(solution)/shard_map/jvp(vmap())/sub | solution.py:117
  109.2 3.4 %fusion.58 = f32[15,2,128,128]{3,2,1,0:T(8,128)S(1)} fusion(f32[15,2,128,128]{3,2,1,0:T(8,128)S(1)} %copy-done.73, f32[16,2,128,128]{2,3,1,0:T(8,128)S(1)} %get-tuple-element.74), kind=kOutput, calls=%fused_computation.104 | convolution fusion | flops 755466240 | bytes 7995392 | tf_op jit(solution)/shard_map/jvp(bhij,bhjk->bhik)/dot_general | solution.py:292
  112.9 3.3 fusion.25
  134.0 3.8 %multiply_reduce_fusion.8 = (f32[16,64,2]{1,2,0:T(2,128)}, f32[16,64,2,128]{3,1,2,0:T(8,128)}) fusion(f32[16,64,128]{2,1,0:T(8,128)S(1)} %bitcast.277, f32[8,2,128,128]{3,2,1,0:T(8,128)S(1)} %convolution_add_fusion.11, f32[8,2,128,128]{3,2,1,0:T(8,128)S(1)} %pad_maximum_fusion.19, bf16[16,64,2,128]{3,2,1,0:T(2,128)(2,1)S(1)} %copy-done.71), kind=kOutput, calls=%fused_computation.163 | convolution fusion | flops 403699712 | bytes 4202496 | tf_op jit(solution)/shard_map/transpose(jvp(vmap(hcd,hde->hce)))/dot_general | solution.py:129
  140.9 3.7 %convolution_add_fusion = f32[16,2,128,128]{3,2,1,0:T(8,128)S(1)} fusion(f32[16,2,128,128]{3,2,1,0:T(8,128)S(1)} %fusion.54, f32[16,2,64,128]{3,2,1,0:T(8,128)S(1)} %fusion.137, f32[16,2,64,256]{3,2,1,0:T(8,128)S(1)} %copy-done.18), kind=kOutput, calls=%fused_computation.76 | convolution fusion | flops 403439616 | bytes 6291456 | tf_op jit(solution)/shard_map/transpose(jvp(vmap(hcd,hde->hce)))/dot_general | solution.py:126
  154.4 5.6 %reverse_add_fusion = f32[15,2,128,128]{3,2,1,0:T(8,128)S(1)} fusion(f32[15,2,128,128]{3,2,1,0:T(8,128)} %slice.378, f32[15,2,128,128]{2,3,1,0:T(8,128)S(1)} %slice.319, f32[16,2,128,128]{3,2,1,0:T(8,128)} %copy-done.25), kind=kOutput, calls=%fused_computation.60 | convolution fusion | flops 755466240 | bytes 7864320 | tf_op jit(solution)/shard_map/transpose(jvp(bhij,bhjk->bhik))/dot_general | solution.py:354
  159.9 4.9 %fusion.21 = f32[15,2,128,128]{3,2,1,0:T(8,128)S(1)} fusion(f32[15,2,128,128]{2,3,1,0:T(8,128)} %copy-done, f32[15,2,128,128]{2,3,1,0:T(8,128)S(1)} %copy-done.74), kind=kOutput, calls=%fused_computation.53 | convolution fusion | flops 754974720 | bytes 5898240 | tf_op jit(solution)/shard_map/transpose(jvp(bhij,bhjk->bhik))/dot_general | solution.py:354
  183.1 5.3 %fusion.13 = f32[16,2,64,128]{3,2,1,0:T(8,128)S(1)} fusion(f32[15,2,128,128]{3,2,1,0:T(8,128)S(1)} %slice.340, f32[16,2,64,256]{3,2,1,0:T(8,128)} %copy-done.17), kind=kOutput, calls=%fused_computation.37 | convolution fusion | flops 402653184 | bytes 4063232 | tf_op jit(solution)/shard_map/transpose(jvp(vmap(hcd,hce->hde)))/dot_general | solution.py:120
  188.4 3.7 %fusion.68 = f32[16,2,64,128]{3,2,1,0:T(8,128)S(1)} fusion(f32[16,2,64,128]{3,2,1,0:T(8,128)S(1)} %copy-done.63, f32[15,2,128,128]{3,2,1,0:T(8,128)} %copy-done.10, f32[16,2,64]{2,1,0:T(2,128)S(1)} %copy-done.95, f32[16,64,128]{2,1,0:T(8,128)S(1)} %bitcast.270), kind=kOutput, calls=%fused_computation.109 | convolution fusion | flops 403177472 | bytes 4595712 | tf_op jit(solution)/shard_map/transpose(jvp(vmap(hcd,hce->hde)))/dot_general | solution.py:120
  192.1 4.6 %fusion.17 = f32[15,2,128,128]{2,3,1,0:T(8,128)S(1)} fusion(f32[15,2,128,128]{3,2,1,0:T(8,128)S(1)} %copy-done.11, f32[8,2,128,128]{3,2,1,0:T(8,128)S(1)} %copy-done.9, f32[8,2,128,128]{3,2,1,0:T(8,128)S(1)} %pad_maximum_fusion.19), kind=kOutput, calls=%fused_computation.48 | convolution fusion | flops 755466240 | bytes 6029312 | tf_op jit(solution)/shard_map/transpose(jvp(bhik,bhjk->bhij))/dot_general | solution.py:354
  196.7 4.1 %fusion.105 = f32[16,2,64,128]{3,2,1,0:T(8,128)S(1)} fusion(f32[16,2,64,128]{3,2,1,0:T(8,128)S(1)} %copy-done.63, f32[8,2,128,128]{3,2,1,0:T(8,128)S(1)} %copy-done.9, f32[8,2,128,128]{3,2,1,0:T(8,128)S(1)} %pad_maximum_fusion.19), kind=kOutput, calls=%fused_computation.170 | convolution fusion | flops 403439616 | bytes 4194304 | tf_op jit(solution)/shard_map/transpose(jvp(vmap(hcd,hde->hce)))/dot_general | solution.py:126
  201.1 4.1 %fusion.73 = f32[16,2,64,128]{3,2,1,0:T(8,128)S(1)} fusion(f32[16,2,64,128]{3,2,1,0:T(8,128)S(1)} %fusion.105, f32[15,2,128,128]{2,3,1,0:T(8,128)S(1)} %fusion.17, f32[16,2,64]{2,1,0:T(2,128)S(1)} %copy-done.95, f32[16,64,128]{2,1,0:T(8,128)S(1)} %bitcast.271), kind=kOutput, calls=%fused_computation.110 | convolution fusion | flops 403701760 | bytes 4595712 | tf_op jit(solution)/shard_map/transpose(jvp(vmap(hcd,hce->hde)))/dot_general | solution.py:117
  270.5 3.6 %multiply_reduce_fusion.2 = (f32[512]{0:T(512)S(1)}, f32[512]{0:T(512)S(1)}, f32[512]{0:T(512)S(1)}, f32[512]{0:T(512)S(1)}, f32[1024,512]{1,0:T(8,128)}) fusion(f32[1024,512]{1,0:T(8,128)S(1)} %copy-done.21, f32[1024]{0:T(1024)S(1)} %copy-done.114, f32[1024]{0:T(1024)S(1)} %copy-done.116, f32[1024]{0:T(1024)S(1)} %copy-done.112, ...), kind=kLoop, calls=%fused_computation.27 | loop fusion | flops 12056576 | bytes 9457664 | tf_op jit(solution)/shard_map/transpose(jvp())/reduce_sum | solution.py:263
  281.4 3.3 all-to-all-start.3
  284.8 3.3 fusion.87
  292.8 4.1 %all-to-all-start.2 = ((bf16[8,128,1,768]{3,1,2,0:T(8,128)(2,1)}), bf16[8,128,1,768]{3,1,2,0:T(8,128)(2,1)S(1)}, u32[]{:S(2)}, u32[]{:S(2)}) async-start(bf16[8,128,1,768]{3,1,2,0:T(8,128)(2,1)} %bitcast.43), calls=%async_computation.2 | async-start | bytes 3145728 | tf_op jit(solution)/shard_map/all_to_all | solution.py:378
  299.1 19.4 %collective-permute-done.1 = f32[4,4096]{1,0:T(4,128)S(1)} collective-permute-done((f32[4,4096]{1,0:T(4,128)S(1)}, f32[4,4096]{1,0:T(4,128)S(1)}, u32[]{:S(2)}, u32[]{:S(2)}) %collective-permute-start.1) | collective-permute-done | bytes 65568 | tf_op jit(solution)/shard_map/ppermute | solution.py:249
  (489 shorter events, 211.3 us)
Async XLA Ops:
  2.6 11.3 %all-to-all-start.1 = ((f32[128,8,5]{0,2,1:T(8,128)}), f32[128,8,5]{0,2,1:T(8,128)S(1)}, u32[]{:S(2)}, u32[]{:S(2)}) async-start(f32[128,8,5]{0,2,1:T(8,128)} %pad_maximum_fusion.25), calls=%async_computation.1 | async-start | bytes 65536 | tf_op jit(solution)/shard_map/all_to_all | solution.py:374
  10.4 71.9 %copy-start.75 = (f32[64,64]{0,1:T(8,128)}, f32[64,64]{0,1:T(8,128)S(1)}, u32[]{:S(2)}) copy-start(f32[64,64]{0,1:T(8,128)S(1)} %fusion.209) | copy-start | bytes 49156
  11.0 101.6 %copy-start.82 = (f32[128,128]{0,1:T(8,128)}, f32[128,128]{0,1:T(8,128)S(1)}, u32[]{:S(2)}) copy-start(f32[128,128]{0,1:T(8,128)S(1)} %get-tuple-element.98) | copy-start | bytes 196612
  14.0 25.2 %all-to-all-start = ((bf16[128,8,768]{0,2,1:T(8,128)(2,1)}), bf16[128,8,768]{0,2,1:T(8,128)(2,1)S(1)}, u32[]{:S(2)}, u32[]{:S(2)}) async-start(bf16[128,8,768]{0,2,1:T(8,128)(2,1)} %pad_maximum_fusion.12), calls=%async_computation | async-start | bytes 3145728 | tf_op jit(solution)/shard_map/all_to_all | solution.py:374
  26.7 42.9 %copy-start.86 = (f32[16,2,64]{2,1,0:T(2,128)}, f32[16,2,64]{2,1,0:T(2,128)S(1)}, u32[]{:S(2)}) copy-start(f32[16,2,64]{2,1,0:T(2,128)S(1)} %copy.461) | copy-start | bytes 24580
  27.6 65.6 %copy-start.94 = (f32[16,2,64]{2,1,0:T(2,128)}, f32[16,2,64]{2,1,0:T(2,128)S(1)}, u32[]{:S(2)}) copy-start(f32[16,2,64]{2,1,0:T(2,128)S(1)} %copy.460) | copy-start | bytes 24580
  30.7 38.9 %copy-start.65 = (pred[16,64,64]{1,2,0:T(8,128)(4,1)}, pred[16,64,64]{1,2,0:T(8,128)(4,1)S(1)}, u32[]{:S(2)}) copy-start(pred[16,64,64]{1,2,0:T(8,128)(4,1)S(1)} %get-tuple-element.76) | copy-start | bytes 196612
  30.7 109.2 %copy-start.80 = (pred[16,64,64]{1,2,0:T(8,128)(4,1)}, pred[16,64,64]{1,2,0:T(8,128)(4,1)S(1)}, u32[]{:S(2)}) copy-start(pred[16,64,64]{1,2,0:T(8,128)(4,1)S(1)} %get-tuple-element.75) | copy-start | bytes 196612
  45.5 92.2 %copy-start.22 = (f32[1024,128]{1,0:T(8,128)}, f32[1024,128]{1,0:T(8,128)S(1)}, u32[]{:S(2)}) copy-start(f32[1024,128]{1,0:T(8,128)S(1)} %get-tuple-element.52) | copy-start | bytes 1572868
  47.4 22.2 %copy-start.1 = (f32[16,2,64,64]{2,3,1,0:T(8,128)}, f32[16,2,64,64]{2,3,1,0:T(8,128)S(1)}, u32[]{:S(2)}) copy-start(f32[16,2,64,64]{2,3,1,0:T(8,128)S(1)} %fusion.172) | copy-start | bytes 1572868
  134.0 5.9 %copy-start.37 = (f32[16,2,64,64]{2,3,1,0:T(8,128)}, f32[16,2,64,64]{2,3,1,0:T(8,128)S(1)}, u32[]{:S(2)}) copy-start(f32[16,2,64,64]{2,3,1,0:T(8,128)S(1)} %fusion.154) | copy-start | bytes 1572868
  154.3 5.6 %copy-start.74 = (f32[15,2,128,128]{2,3,1,0:T(8,128)S(1)}, f32[15,2,128,128]{2,3,1,0:T(8,128)}, u32[]{:S(2)}) copy-start(f32[15,2,128,128]{2,3,1,0:T(8,128)} %fusion.359) | copy-start | bytes 5898244
  183.1 5.3 %copy-start.63 = (f32[16,2,64,128]{3,2,1,0:T(8,128)S(1)}, f32[16,2,64,128]{3,2,1,0:T(8,128)}, u32[]{:S(2)}) copy-start(f32[16,2,64,128]{3,2,1,0:T(8,128)} %copy-done.62) | copy-start | bytes 3145732
  183.1 5.3 %copy-start.95 = (f32[16,2,64]{2,1,0:T(2,128)S(1)}, f32[16,2,64]{2,1,0:T(2,128)}, u32[]{:S(2)}) copy-start(f32[16,2,64]{2,1,0:T(2,128)} %copy-done.94) | copy-start | bytes 24580
  207.4 9.4 %copy-start.67 = (f32[16,64,2,256]{3,1,2,0:T(8,128)}, f32[16,64,2,256]{3,1,2,0:T(8,128)S(1)}, u32[]{:S(2)}) copy-start(f32[16,64,2,256]{3,1,2,0:T(8,128)S(1)} %fusion.40) | copy-start | bytes 6291460
  209.8 5.1 %copy-start.60 = (f32[16,2,64,128]{3,2,1,0:T(8,128)S(1)}, f32[16,2,64,128]{3,2,1,0:T(8,128)}, u32[]{:S(2)}) copy-start(f32[16,2,64,128]{3,2,1,0:T(8,128)} %convolution_subtract_fusion) | copy-start | bytes 3145732
  277.4 7.4 %copy-start.101 = (f32[16,2,64]{2,1,0:T(2,128)S(1)}, f32[16,2,64]{2,1,0:T(2,128)}, u32[]{:S(2)}) copy-start(f32[16,2,64]{2,1,0:T(2,128)} %copy.458) | copy-start | bytes 24580
  277.6 19.4 %collective-permute-start = (f32[4,4096]{1,0:T(4,128)S(1)}, f32[4,4096]{1,0:T(4,128)S(1)}, u32[]{:S(2)}, u32[]{:S(2)}) collective-permute-start(f32[4,4096]{1,0:T(4,128)S(1)} %constant_dynamic-update-slice_fusion), channel_id=1, source_target_pairs={{0,1},{1,0},{2,3},{3,2},{4,5},{5,4},{6,7},{7,6},{8,9},{9,8},{10,11... | collective-permute-start | bytes 196616 | tf_op jit(solution)/shard_map/ppermute | solution.py:249
  281.4 11.4 %all-to-all-start.3 = ((f32[8,128,1,4]{1,3,2,0:T(4,128)}), f32[8,128,1,4]{1,3,2,0:T(4,128)S(1)}, u32[]{:S(2)}, u32[]{:S(2)}) async-start(f32[8,128,1,4]{1,3,2,0:T(4,128)} %copy.544), calls=%async_computation.3 | async-start | bytes 32768 | tf_op jit(solution)/shard_map/all_to_all | solution.py:378
  292.8 40.2 %all-to-all-start.2 = ((bf16[8,128,1,768]{3,1,2,0:T(8,128)(2,1)}), bf16[8,128,1,768]{3,1,2,0:T(8,128)(2,1)S(1)}, u32[]{:S(2)}, u32[]{:S(2)}) async-start(bf16[8,128,1,768]{3,1,2,0:T(8,128)(2,1)} %bitcast.43), calls=%async_computation.2 | async-start | bytes 3145728 | tf_op jit(solution)/shard_map/all_to_all | solution.py:378
  297.0 21.5 %collective-permute-start.1 = (f32[4,4096]{1,0:T(4,128)S(1)}, f32[4,4096]{1,0:T(4,128)S(1)}, u32[]{:S(2)}, u32[]{:S(2)}) collective-permute-start(f32[4,4096]{1,0:T(4,128)S(1)} %add.184), channel_id=1, source_target_pairs={{0,2},{1,3},{2,0},{3,1},{4,6},{5,7},{6,4},{7,5},{8,10},{9,11},{10,... | collective-permute-start | bytes 196616 | tf_op jit(solution)/shard_map/ppermute | solution.py:249
  318.5 4.3 %collective-permute-start.2 = (f32[4,4096]{1,0:T(4,128)S(1)}, f32[4,4096]{1,0:T(4,128)S(1)}, u32[]{:S(2)}, u32[]{:S(2)}) collective-permute-start(f32[4,4096]{1,0:T(4,128)S(1)} %add.185), channel_id=1, source_target_pairs={{0,4},{1,5},{2,6},{3,7},{4,0},{5,1},{6,2},{7,3},{8,12},{9,13},{10,... | collective-permute-start | bytes 196616 | tf_op jit(solution)/shard_map/ppermute | solution.py:249
  322.8 4.3 %collective-permute-start.3 = (f32[4,4096]{1,0:T(4,128)S(1)}, f32[4,4096]{1,0:T(4,128)S(1)}, u32[]{:S(2)}, u32[]{:S(2)}) collective-permute-start(f32[4,4096]{1,0:T(4,128)S(1)} %add.186), channel_id=1, source_target_pairs={{0,8},{8,0},{16,24},{24,16},{1,9},{9,1},{17,25},{25,17},{2,10},{10... | collective-permute-start | bytes 196616 | tf_op jit(solution)/shard_map/ppermute | solution.py:249
  327.2 5.2 %collective-permute-start.4 = (f32[4,4096]{1,0:T(4,128)S(1)}, f32[4,4096]{1,0:T(4,128)S(1)}, u32[]{:S(2)}, u32[]{:S(2)}) collective-permute-start(f32[4,4096]{1,0:T(4,128)S(1)} %add.187), channel_id=1, source_target_pairs={{0,16},{8,24},{16,0},{24,8},{1,17},{9,25},{17,1},{25,9},{2,18},{10... | collective-permute-start | bytes 196616 | tf_op jit(solution)/shard_map/ppermute | solution.py:249
  (129 other events, 342.2 us)
